TPU v7x, 512 devices: a whole 4x4x16 slice. The times are simulated.
512 devices in a mesh: dp: 4 (over x), seq: 8 (over z_lo), tensor: 16 (over z_hi, y, core).
Axes of the slice: x: 4, y: 4, z: 16 (z_hi: 2, z_lo: 8; z = z_hi * 8 + z_lo), core: 2. Of those that a mesh axis runs over, the one named last changes fastest.
Arguments:
- features: bfloat16 [4096, 4096], P(('dp', 'seq'), 'tensor'), parts along dimension 0, may hold values from -6 to 6
- in_weight: bfloat16 [4096, 3, 4096], P('seq', None, 'tensor'), may hold values from -0.09375 to 0.09375
- short_taps: float32 [3, 7, 4096], P(None, None, 'tensor'), may hold values from -2.5 to 2.5
- decay_rates: float32 [16, 4096], P(None, 'tensor'), may hold values from 0.00048828125 to 0.1
- residues: float32 [16, 4096], P(None, 'tensor'), may hold values from -1.5 to 1.5
- skip_gain: float32 [4096], P('tensor'), may hold values from 0.5 to 1.5
- out_weight: bfloat16 [4096, 4096], P(None, 'tensor'), may hold values from -0.09375 to 0.09375
Outputs:
- mixed: bfloat16 [4096, 4096], P(('dp', 'seq'), 'tensor'), parts along dimension 0
There are 4 independent parts, one for each index of `dp`. A program takes and returns all parts, laid end to end along the dimension named above; an argument that names none is the same for every part. Nothing has to cross between parts.
All inputs are finite; a program needn't handle non-finite values.
Results may differ from a plain program's by a relative error of at most 0.007.
Values may be sent and summed in bfloat16 or wider, within the bound.
No kernel may reach another device: no remote copies, remote signals or barrier semaphores. Data moves between devices by JAX's collectives and lax.ppermute only.
A program may use at most 64 MiB of HBM per device.

v0:
```python
import jax
import jax.numpy as jnp
from jax import lax
from jax.sharding import PartitionSpec as P

precise = lax.Precision.HIGHEST
block_len = 64


def passed_along(value, axis, steps):
    count = lax.axis_size(axis)
    leading, last = (max(0, -steps), min(count, count - steps))
    return lax.ppermute(value, axis, [(source, source + steps) for source in range(leading, last)])


def body(features, in_weight, short_taps, decay_rates, residues, skip_gain, out_weight):
    tok_rows = features.shape[0]
    channels = in_weight.shape[2]
    taps_count = short_taps.shape[1]
    whole_feats = lax.all_gather(features, "tensor", axis=1, tiled=True)
    piece = lax.all_gather(in_weight, "seq", axis=0, tiled=True)
    count = piece.shape[0]
    projected = jnp.dot(
        whole_feats, piece.reshape(count, 3 * channels), preferred_element_type=jnp.float32
    )
    projected = projected.astype(jnp.bfloat16).reshape(tok_rows, 3, channels)
    rim_rows = taps_count - 1
    earlier = passed_along(projected[tok_rows - rim_rows :], "seq", 1)
    extended = jnp.concatenate([earlier, projected], axis=0).astype(jnp.float32)
    short = jnp.zeros((tok_rows, 3, channels), jnp.float32)
    for offset_lag in range(taps_count):
        short = (
            short
            + short_taps[:, offset_lag, :][None]
            * extended[rim_rows - offset_lag : rim_rows - offset_lag + tok_rows]
        )
    product = short[:, 1, :] * short[:, 2, :]
    blocks = tok_rows // block_len
    pieces = product.reshape(blocks, block_len, channels)
    amplitude = residues * jnp.sqrt(2.0 * decay_rates)
    offsets = jnp.arange(block_len).astype(jnp.float32)
    falloff = jnp.exp(-decay_rates[:, None, :] * offsets[None, :, None])
    kernel = jnp.einsum("mc,mtc->tc", amplitude, falloff, precision=precise)
    lag_grid = jnp.arange(block_len)[:, None] - jnp.arange(block_len)[None, :]
    select = (lag_grid[:, :, None] == jnp.arange(block_len)[None, None, :]).astype(jnp.float32)
    toeplitz = jnp.einsum("tsk,kc->tsc", select, kernel, precision=precise)
    inner = jnp.einsum("tsc,bsc->btc", toeplitz, pieces, precision=precise)
    toward_end = jnp.exp(-decay_rates[:, None, :] * (block_len - offsets)[None, :, None])
    block_sums = jnp.einsum("msc,bsc->bmc", toward_end, pieces, precision=precise)
    block_index = jnp.arange(blocks).astype(jnp.float32)
    carry_over = jnp.exp(
        -decay_rates[None] * (block_len * (blocks - 1 - block_index))[:, None, None]
    )
    device_sum = jnp.sum(carry_over * block_sums, axis=0)
    place = lax.axis_index("seq")
    gathered_sums = lax.all_gather(device_sum, "seq")
    earlier_count = jnp.arange(gathered_sums.shape[0])
    distance = (place - 1 - earlier_count).astype(jnp.float32)
    weight = jnp.where(
        (earlier_count < place)[:, None, None],
        jnp.exp(-decay_rates[None] * (float(tok_rows) * jnp.maximum(distance, 0.0))[:, None, None]),
        0.0,
    )
    entering = jnp.sum(weight * gathered_sums, axis=0)
    step_decay = jnp.exp(-decay_rates * float(block_len))

    def advance(state, block_sum):
        return (step_decay * state + block_sum, state)

    final_state, starts = lax.scan(advance, entering, block_sums)
    outer = jnp.einsum("mic,bmc->bic", amplitude[:, None, :] * falloff, starts, precision=precise)
    conv = (inner + outer).reshape(tok_rows, channels)
    gated = (short[:, 0, :] * (conv + skip_gain[None, :] * product)).astype(jnp.bfloat16)
    mixed = jnp.dot(
        lax.all_gather(gated, "tensor", axis=1, tiled=True),
        out_weight,
        preferred_element_type=jnp.float32,
    )
    return mixed.astype(jnp.bfloat16)


def solution(mesh):
    in_specs = (
        P(("dp", "seq"), "tensor"),
        P("seq", None, "tensor"),
        P(None, None, "tensor"),
        P(None, "tensor"),
        P(None, "tensor"),
        P("tensor"),
        P(None, "tensor"),
    )
    out_specs = P(("dp", "seq"), "tensor")
    return jax.shard_map(body, mesh=mesh, in_specs=in_specs, out_specs=out_specs, check_vma=False)
```

profile of v0, /device:TPU:1, one launch (start us, length us, event | category | flops | bytes accessed | tf_op | source)
XLA Modules:
  0.0 405.0 jit_solution(2613455563154956939)
XLA Ops:
  6.5 0.0 copy-start
  6.5 0.0 copy-start.2
  6.5 0.0 copy-start.3
  6.5 0.0 copy-start.1
  6.5 0.0 all-gather.5.cloned.1.call-start
  6.6 0.7 all-gather.5.cloned.1.call-update
  7.3 0.0 all-gather.7.cloned.1.call-start
  7.3 2.3 copy.59
  9.6 0.0 all-gather.7.cloned.1.call-update
  9.7 0.0 all-gather.9.cloned.1.call-start
  9.7 0.0 copy-done.2
  9.7 0.0 copy-done.3
  9.7 0.1 copy.63
  9.8 0.1 copy.90
  10.0 1.6 multiply_reduce_fusion
  11.6 0.0 copy-done.1
  11.7 3.8 fusion.5
  15.6 77.7 %all-gather.5.cloned.1.call-done = bf16[128,4096]{1,0:T(8,128)(2,1)} async-done(((bf16[128,256]{1,0:T(8,128)(2,1)}), bf16[128,4096]{1,0:T(8,128)(2,1)}) %all-gather.5.cloned.1.call-update) | async-done | bytes 1048592 | tf_op jit(solution)/shard_map/all_gather | solution.py:20
  93.3 135.5 %all-gather.7.cloned.1.call-done = bf16[4096,3,256]{0,2,1:T(8,128)(2,1)} async-done(((bf16[512,3,256]{0,2,1:T(8,128)(2,1)}), bf16[4096,3,256]{0,2,1:T(8,128)(2,1)}) %all-gather.7.cloned.1.call-update) | async-done | bytes 6291472 | tf_op jit(solution)/shard_map/all_gather | solution.py:21
  228.8 5.3 %convolution_convert_fusion = bf16[128,768]{1,0:T(8,128)(2,1)S(1)} fusion(bf16[128,4096]{1,0:T(8,128)(2,1)} %all-gather.5.cloned.1.call-done, bf16[4096,768]{0,1:T(8,128)(2,1)} %bitcast.59), kind=kOutput, calls=%fused_computation.11 | convolution fusion | flops 805404672 | bytes 7536640 | tf_op jit(solution)/shard_map/dot_general | solution.py:23
  234.2 0.2 copy.81
  234.4 1.5 collective-permute-start
  235.9 0.7 copy.70
  236.6 9.2 %copy.65 = f32[64,64,256]{1,0,2:T(8,128)} copy(f32[64,64,256]{2,1,0:T(8,128)} %fusion.5) | data formatting | bytes 8388608 | tf_op jit(solution)/shard_map/tsk,kc->tsc/dot_general | solution.py:46
  245.8 0.2 copy.61
  245.9 0.0 collective-permute-done
  246.0 0.2 maximum_convert_fusion
  246.1 1.5 fusion.21
  247.7 0.1 copy.62
  247.8 0.1 copy.64
  247.9 15.4 %fusion.32 = f32[256,2,64]{2,1,0:T(2,128)S(1)} fusion(f32[2,64,256]{1,0,2:T(2,128)S(1)} %copy.64, f32[64,64,256]{1,0,2:T(8,128)} %copy.65), kind=kOutput, calls=%fused_computation.61 | convolution fusion | flops 25165824 | bytes 4456448 | tf_op jit(solution)/shard_map/tsc,bsc->btc/dot_general | solution.py:47
  263.3 4.2 %multiply_reduce_fusion.1 = (f32[16,256]{0,1:T(8,128)}, f32[2,16,256]{1,0,2:T(2,128)S(1)}) fusion(f32[16,256]{0,1:T(8,128)S(1)} %copy.63, f32[2]{0:T(128)S(1)} %subtract_multiply_fusion, f32[2,64,256]{1,0,2:T(2,128)S(1)} %copy.64, f32[64]{0:T(128)S(1)} %broadcast_subtract_fusion), kind=kOutput, calls=%fused_computation.36 | convolution fusion | flops 6574080 | bytes 196872 | tf_op jit(solution)/shard_map/msc,bsc->bmc/dot_general | solution.py:49
  267.5 1.0 copy.68
  268.5 40.2 %all-gather = f32[128,256]{1,0:T(8,128)S(1)} all-gather(f32[16,256]{1,0:T(8,128)S(1)} %copy.68), channel_id=2, replica_groups=mesh['dp'=4,'seq'=8,'tensor'=16] {'seq'}, dimensions={0}, use_global_device_ids=true | all-gather | bytes 147456 | tf_op jit(solution)/shard_map/all_gather | solution.py:56
  308.7 0.1 copy.69
  308.8 0.1 multiply_reduce_fusion.2
  308.9 0.1 while.12
  309.0 0.1 copy.71
  309.2 0.0 copy-start.4
  309.2 3.7 fusion.12
  312.9 0.1 copy.72
  313.0 0.1 copy.73
  313.1 0.0 copy-done.4
  313.1 0.7 fusion.28
  313.9 0.0 all-gather.9.cloned.1.call-update
  313.9 82.1 %all-gather.9.cloned.1.call-done = bf16[128,4096]{0,1:T(8,128)(2,1)} async-done(((bf16[128,256]{0,1:T(8,128)(2,1)}), bf16[128,4096]{0,1:T(8,128)(2,1)}) %all-gather.9.cloned.1.call-update) | async-done | bytes 1048592 | tf_op jit(solution)/shard_map/all_gather | solution.py:75
  396.0 0.0 copy-done
  396.0 2.4 convolution_convert_fusion.1
  (19 shorter events, 0.1 us)
Async XLA Ops:
  6.5 389.5 %copy-start = (bf16[4096,256]{1,0:T(8,128)(2,1)S(1)}, bf16[4096,256]{1,0:T(8,128)(2,1)}, u32[]{:S(2)}) copy-start(bf16[4096,256]{1,0:T(8,128)(2,1)} %param.15) | copy-start | bytes 6291460
  6.5 3.2 copy-start.2
  6.5 3.2 copy-start.3
  6.5 5.1 %copy-start.1 = (f32[3,7,256]{2,1,0:T(8,128)S(1)}, f32[3,7,256]{2,1,0:T(8,128)}, u32[]{:S(2)}) copy-start(f32[3,7,256]{2,1,0:T(8,128)} %param.11) | copy-start | bytes 64516
  6.5 86.7 %all-gather.5.cloned.1.call-start = ((), (), s32[]{:S(2)}) async-start(), calls=%async_computation | async-start | bytes 1114112 | tf_op jit(solution)/shard_map/all_gather | solution.py:20
  7.3 221.6 %all-gather.7.cloned.1.call-start = ((), (), s32[]{:S(2)}) async-start(), calls=%async_computation.1 | async-start | bytes 7077888 | tf_op jit(solution)/shard_map/all_gather | solution.py:21
  9.7 386.4 %all-gather.9.cloned.1.call-start = ((), (), s32[]{:S(2)}) async-start(), calls=%async_computation.2 | async-start | bytes 1114112 | tf_op jit(solution)/shard_map/all_gather | solution.py:75
  234.4 11.6 %collective-permute-start = (bf16[6,3,256]{0,2,1:T(8,128)(2,1)S(1)}, bf16[6,3,256]{0,2,1:T(8,128)(2,1)S(1)}, u32[]{:S(2)}, u32[]{:S(2)}) collective-permute-start(bf16[6,3,256]{0,2,1:T(8,128)(2,1)S(1)} %bitcast.64), channel_id=1, source_target_pairs={{0,16},{16,32},{32,48},{48,64},{64,80},{80,96},{96,112},{1,17},{17... | collective-permute-start | bytes 27656 | tf_op jit(solution)/shard_map/ppermute | solution.py:13
  309.2 3.9 copy-start.4
Sparse Core Ops, SparseCore 0:
  10.5 82.7 all-gather.4
  95.4 133.4 all-gather.6
  314.0 81.9 all-gather.8
where the time goes:
time: 405 us
  waiting for transfers between devices  296 us (73%)
  blocking collectives  40.2 us (10%)
  matrix products  34.9 us (9%)
  local copies, waits for them, and re-layouts  14.5 us (4%)
  between operations  13.4 us (3%)
  other arithmetic  4.23 us (1%)
    all_gather x1, waiting for transfers between devices, body(): piece = lax.all_gather(in_weight, 'seq', axis=0, tiled=True)  136 us
    all_gather x1, waiting for transfers between devices, body(): lax.all_gather(gated, 'tensor', axis=1, tiled=True)  82.1 us
    all_gather x1, waiting for transfers between devices, body(): whole_feats = lax.all_gather(features, 'tensor', axis=1, tiled=True)  77.7 us
    all_gather x1, blocking collectives, body(): gathered_sums = lax.all_gather(device_sum, 'seq')  40.2 us
    dot_general x1, matrix products, body(): inner = jnp.einsum('tsc,bsc->btc', toeplitz, pieces, precision=precise)  15.4 us
    dot_general x1, local copies, waits for them, and re-layouts, body(): toeplitz = jnp.einsum('tsk,kc->tsc', select, kernel, precision=precise)  9.15 us
  transfers between devices with their start and end apart: 4, of which 3 were waited for; matrix products, arithmetic and copies ran while one was open for 4% of the time, Pallas kernels for 0%

commit v1 on v0

--- a/solution.py
+++ b/solution.py
@@ -5,6 +5,13 @@
 
 precise = lax.Precision.HIGHEST
 block_len = 64
+
+
+def write_the_pieces_all(arr):
+    vec_out = jnp.concatenate(
+        lax.all_to_all(jnp.stack(lax.psum(1, "tensor") * [arr]), "tensor", 0, 0), axis=1
+    )
+    return vec_out
 
 
 def passed_along(value, axis, steps):
@@ -71,11 +78,7 @@
     outer = jnp.einsum("mic,bmc->bic", amplitude[:, None, :] * falloff, starts, precision=precise)
     conv = (inner + outer).reshape(tok_rows, channels)
     gated = (short[:, 0, :] * (conv + skip_gain[None, :] * product)).astype(jnp.bfloat16)
-    mixed = jnp.dot(
-        lax.all_gather(gated, "tensor", axis=1, tiled=True),
-        out_weight,
-        preferred_element_type=jnp.float32,
-    )
+    mixed = jnp.dot(write_the_pieces_all(gated), out_weight, preferred_element_type=jnp.float32)
     return mixed.astype(jnp.bfloat16)
 
 

time: 405 us -> 386 us (0.953)
  waiting for transfers between devices: 296 us -> 214 us
  blocking collectives: 40.2 us -> 104 us
    all_gather x1 -> x0, waiting for transfers between devices: 82.1 us -> none  [body(): lax.all_gather(gated, 'tensor', axis=1, tiled=True)]
    all_to_all x0 -> x1, blocking collectives: none -> 63.8 us  [write_the_pieces_all(): lax.all_to_all(jnp.stack(lax.psum(1, 'tensor') * [arr]), 'tensor', 0, 0)]
  transfers between devices with their start and end apart: 4 -> 3, of which waited for: 3 -> 2; matrix products, arithmetic and copies ran while one was open for 4% -> 5% of each run, Pallas kernels for 0% -> 0%
where the time goes in v1:
time: 386 us; the launch traced here: 385 us
  waiting for transfers between devices  214 us (55%)
  blocking collectives  104 us (27%)
  matrix products  33.7 us (9%)
  local copies, waits for them, and re-layouts  14.7 us (4%)
  between operations  13.7 us (4%)
    all_gather x1, waiting for transfers between devices, body(): piece = lax.all_gather(in_weight, 'seq', axis=0, tiled=True)  136 us
    all_gather x1, waiting for transfers between devices, body(): whole_feats = lax.all_gather(features, 'tensor', axis=1, tiled=True)  77.8 us
    all_to_all x1, blocking collectives, write_the_pieces_all(): lax.all_to_all(jnp.stack(lax.psum(1, 'tensor') * [arr]), 'tensor', 0, 0)  63.8 us
    all_gather x1, blocking collectives, body(): gathered_sums = lax.all_gather(device_sum, 'seq')  40.2 us
    dot_general x1, matrix products, body(): inner = jnp.einsum('tsc,bsc->btc', toeplitz, pieces, precision=precise)  15.4 us
    dot_general x1, local copies, waits for them, and re-layouts, body(): toeplitz = jnp.einsum('tsk,kc->tsc', select, kernel, precision=precise)  9.13 us
  transfers between devices with their start and end apart: 3, of which 2 were waited for; matrix products, arithmetic and copies ran while one was open for 5% of the time, Pallas kernels for 0%

profile of v1, /device:TPU:1, one launch (start us, length us, event | category | flops | bytes accessed | tf_op | source)
XLA Modules:
  0.0 385.3 jit_solution(14007306058301052159)
XLA Ops:
  6.5 0.0 copy-start
  6.5 0.0 copy-start.2
  6.5 0.0 copy-start.3
  6.5 0.0 copy-start.1
  6.5 0.0 all-gather.4.cloned.1.call-start
  6.6 0.7 all-gather.4.cloned.1.call-update
  7.3 0.0 all-gather.6.cloned.1.call-start
  7.3 2.3 copy.59
  9.6 0.0 all-gather.6.cloned.1.call-update
  9.7 0.0 copy-done.2
  9.7 0.0 copy-done.3
  9.7 0.1 copy.90
  9.8 0.1 copy.63
  10.0 1.6 multiply_reduce_fusion
  11.6 0.0 copy-done.1
  11.7 3.9 %fusion.5 = f32[64,64,256]{2,1,0:T(8,128)} fusion(s32[64,64]{1,0:T(8,128)S(1)} %iota_subtract_fusion, f32[256,64]{1,0:T(8,128)S(1)} %multiply_reduce_fusion), kind=kOutput, calls=%fused_computation.10 | convolution fusion | flops 805568512 | bytes 4276224 | tf_op jit(solution)/shard_map/tsk,kc->tsc/dot_general | solution.py:53
  15.5 77.8 %all-gather.4.cloned.1.call-done = bf16[128,4096]{1,0:T(8,128)(2,1)} async-done(((bf16[128,256]{1,0:T(8,128)(2,1)}), bf16[128,4096]{1,0:T(8,128)(2,1)}) %all-gather.4.cloned.1.call-update) | async-done | bytes 1048592 | tf_op jit(solution)/shard_map/all_gather | solution.py:27
  93.3 135.5 %all-gather.6.cloned.1.call-done = bf16[4096,3,256]{0,2,1:T(8,128)(2,1)} async-done(((bf16[512,3,256]{0,2,1:T(8,128)(2,1)}), bf16[4096,3,256]{0,2,1:T(8,128)(2,1)}) %all-gather.6.cloned.1.call-update) | async-done | bytes 6291472 | tf_op jit(solution)/shard_map/all_gather | solution.py:28
  228.8 5.3 %convolution_convert_fusion = bf16[128,768]{1,0:T(8,128)(2,1)S(1)} fusion(bf16[128,4096]{1,0:T(8,128)(2,1)} %all-gather.4.cloned.1.call-done, bf16[4096,768]{0,1:T(8,128)(2,1)} %bitcast.62), kind=kOutput, calls=%fused_computation.11 | convolution fusion | flops 805404672 | bytes 7536640 | tf_op jit(solution)/shard_map/dot_general | solution.py:30
  234.2 0.2 copy.81
  234.4 1.5 collective-permute-start
  235.9 0.8 copy.70
  236.6 9.1 %copy.65 = f32[64,64,256]{1,0,2:T(8,128)} copy(f32[64,64,256]{2,1,0:T(8,128)} %fusion.5) | data formatting | bytes 8388608 | tf_op jit(solution)/shard_map/tsk,kc->tsc/dot_general | solution.py:53
  245.8 0.2 copy.61
  245.9 0.0 collective-permute-done
  245.9 0.2 maximum_convert_fusion
  246.1 1.5 fusion.21
  247.6 0.1 copy.62
  247.7 0.1 copy.64
  247.9 15.4 %fusion.32 = f32[256,2,64]{2,1,0:T(2,128)S(1)} fusion(f32[2,64,256]{1,0,2:T(2,128)S(1)} %copy.64, f32[64,64,256]{1,0,2:T(8,128)} %copy.65), kind=kOutput, calls=%fused_computation.61 | convolution fusion | flops 25165824 | bytes 4456448 | tf_op jit(solution)/shard_map/tsc,bsc->btc/dot_general | solution.py:54
  263.3 4.2 %multiply_reduce_fusion.1 = (f32[16,256]{0,1:T(8,128)}, f32[2,16,256]{1,0,2:T(2,128)S(1)}) fusion(f32[16,256]{0,1:T(8,128)S(1)} %copy.63, f32[2]{0:T(128)S(1)} %subtract_multiply_fusion, f32[2,64,256]{1,0,2:T(2,128)S(1)} %copy.64, f32[64]{0:T(128)S(1)} %broadcast_subtract_fusion), kind=kOutput, calls=%fused_computation.36 | convolution fusion | flops 6574080 | bytes 196872 | tf_op jit(solution)/shard_map/msc,bsc->bmc/dot_general | solution.py:56
  267.5 1.0 copy.68
  268.5 40.2 %all-gather = f32[128,256]{1,0:T(8,128)S(1)} all-gather(f32[16,256]{1,0:T(8,128)S(1)} %copy.68), channel_id=2, replica_groups=mesh['dp'=4,'seq'=8,'tensor'=16] {'seq'}, dimensions={0}, use_global_device_ids=true | all-gather | bytes 147456 | tf_op jit(solution)/shard_map/all_gather | solution.py:63
  308.7 0.1 copy.69
  308.8 0.1 multiply_reduce_fusion.2
  308.9 0.1 while.12
  309.0 0.1 copy.71
  309.1 0.0 copy-start.4
  309.1 3.7 fusion.12
  312.9 0.1 copy.72
  313.0 0.1 copy.73
  313.1 0.0 copy-done.4
  313.1 0.1 fusion.28
  313.2 0.2 stack.2
  313.4 63.8 %all_to_all.5 = bf16[16,128,256]{1,2,0:T(8,128)(2,1)S(1)} all-to-all(bf16[16,128,256]{1,2,0:T(8,128)(2,1)S(1)} %stack.2), channel_id=1, replica_groups=mesh['dp'=4,'seq'=8,'tensor'=16] {'tensor'}, dimensions={0} | all-to-all | bytes 2097152 | tf_op jit(solution)/shard_map/all_to_all | solution.py:12
  377.2 0.0 copy-done
  377.2 1.2 convolution_convert_fusion.1
  (19 shorter events, 0.1 us)
Async XLA Ops:
  6.5 370.7 %copy-start = (bf16[4096,256]{1,0:T(8,128)(2,1)S(1)}, bf16[4096,256]{1,0:T(8,128)(2,1)}, u32[]{:S(2)}) copy-start(bf16[4096,256]{1,0:T(8,128)(2,1)} %param.15) | copy-start | bytes 6291460
  6.5 3.1 copy-start.2
  6.5 3.1 copy-start.3
  6.5 5.0 %copy-start.1 = (f32[3,7,256]{2,1,0:T(8,128)S(1)}, f32[3,7,256]{2,1,0:T(8,128)}, u32[]{:S(2)}) copy-start(f32[3,7,256]{2,1,0:T(8,128)} %param.11) | copy-start | bytes 64516
  6.5 86.7 %all-gather.4.cloned.1.call-start = ((), (), s32[]{:S(2)}) async-start(), calls=%async_computation.1 | async-start | bytes 1114112 | tf_op jit(solution)/shard_map/all_gather | solution.py:27
  7.3 221.5 %all-gather.6.cloned.1.call-start = ((), (), s32[]{:S(2)}) async-start(), calls=%async_computation.2 | async-start | bytes 7077888 | tf_op jit(solution)/shard_map/all_gather | solution.py:28
  234.4 11.6 %collective-permute-start = (bf16[6,3,256]{0,2,1:T(8,128)(2,1)S(1)}, bf16[6,3,256]{0,2,1:T(8,128)(2,1)S(1)}, u32[]{:S(2)}, u32[]{:S(2)}) collective-permute-start(bf16[6,3,256]{0,2,1:T(8,128)(2,1)S(1)} %bitcast.68), channel_id=1, source_target_pairs={{0,16},{16,32},{32,48},{48,64},{64,80},{80,96},{96,112},{1,17},{17... | collective-permute-start | bytes 27656 | tf_op jit(solution)/shard_map/ppermute | solution.py:20
  309.1 3.9 %copy-start.4 = (f32[256]{0:T(256)S(1)}, f32[256]{0:T(256)}, u32[]{:S(2)}) copy-start(f32[256]{0:T(256)} %param.14) | copy-start | bytes 3076
Sparse Core Ops, SparseCore 0:
  10.5 82.7 all-gather.3
  95.4 133.4 all-gather.5
